TPU v7x, 128 devices: a whole 4x4x4 slice. The times are simulated.
128 devices in a mesh: batch: 8 (over y, core), seq: 16 (over x, z).
Axes of the slice: x: 4, y: 4, z: 4, core: 2. Of those that a mesh axis runs over, the one named last changes fastest.
Arguments:
- frames: bfloat16 [8, 3072, 1024], P('batch', 'seq'), may hold values from -6 to 6
- lengths: int32 [8], P('batch'), may hold values from 768 to 3072, as said below
- w_qkv: bfloat16 [1024, 3072], replicated, may hold values from -0.25 to 0.25
- w_out: bfloat16 [1024, 1024], replicated, may hold values from -0.1875 to 0.1875
- cotangent: bfloat16 [8, 3072, 1024], P('batch', 'seq'), may hold values from -6 to 6
Outputs:
- output: bfloat16 [8, 3072, 1024], P('batch', 'seq')
- grad_input: bfloat16 [8, 3072, 1024], P('batch', 'seq')
- grad_qkv: float32 [1024, 3072], P('seq')
- grad_out: float32 [1024, 1024], P('seq')
Inputs may be any that keep to these rules, and one draw needn't show every extreme that they name: `lengths`: at least one utterance has all 3072 frames valid.
All inputs are finite; a program needn't handle non-finite values.
Results may differ from a plain program's by a relative error of at most 0.012.
The roundings to bfloat16 on the way count: a program that leaves them out, or rounds other values in their place, can miss the bound.
Values may be sent and summed in bfloat16 or wider, within the bound.
No kernel may reach another device: no remote copies, remote signals or barrier semaphores. Data moves between devices by JAX's collectives and lax.ppermute only.
A program may use at most 128 MiB of HBM per device.

v0:
```python
import jax
import jax.numpy as jnp
from jax import lax
from jax.sharding import PartitionSpec as P

H = 8


def from_partner(array, axis, stride):
    return lax.ppermute(array, axis, [(i, i ^ 1 << stride) for i in range(lax.axis_size(axis))])


def layer_norm(values):
    mean = jnp.mean(values, axis=-1, keepdims=True)
    centred = values - mean
    var = jnp.mean(centred * centred, axis=-1, keepdims=True)
    return centred * lax.rsqrt(var + 1e-05)


def block_forward(query_rows, keys, values, bias, scale):
    scores = jnp.dot(query_rows, keys.T, preferred_element_type=jnp.float32) * scale + bias[None, :]
    top = jnp.max(scores, axis=1, keepdims=True)
    expo = jnp.exp(scores - top)
    probs = expo / jnp.sum(expo, axis=1, keepdims=True)
    p_half = probs.astype(jnp.bfloat16)
    return (probs, p_half, jnp.dot(p_half, values, preferred_element_type=jnp.float32))


def head_backward(query, keys, values, dcontext, bias, scale):
    total, width = query.shape
    rows = min(512, total)
    qblocks = query.reshape(total // rows, rows, width)
    dblocks = dcontext.reshape(total // rows, rows, width)
    key_count = keys.shape[0]

    def step(carry, item):
        dkeys, dvalues = carry
        query_rows, d_rows = item
        probs, p_half, unused = block_forward(query_rows, keys, values, bias, scale)
        dprobs = jnp.dot(d_rows, values.T, preferred_element_type=jnp.float32)
        delta = jnp.sum(probs * dprobs, axis=1, keepdims=True)
        dscores = (probs * (dprobs - delta)).astype(jnp.bfloat16)
        dquery = jnp.dot(dscores, keys, preferred_element_type=jnp.float32) * scale
        dkeys = dkeys + jnp.dot(dscores.T, query_rows, preferred_element_type=jnp.float32) * scale
        dvalues = dvalues + jnp.dot(p_half.T, d_rows, preferred_element_type=jnp.float32)
        return ((dkeys, dvalues), dquery.astype(jnp.bfloat16))

    start = (jnp.zeros((key_count, width), jnp.float32), jnp.zeros((key_count, width), jnp.float32))
    (dkeys, dvalues), dquery = lax.scan(step, start, (qblocks, dblocks))
    return (dquery.reshape(total, width), dkeys, dvalues)


def to_heads(rows_array, groups, head_blocks):
    tok_rows, heads, head_size = rows_array.shape
    local_heads = heads // head_blocks
    part_rows = tok_rows // groups
    shaped = rows_array.reshape(groups, part_rows, head_blocks, local_heads, head_size)
    return shaped.transpose(2, 0, 1, 3, 4).reshape(
        head_blocks * groups, part_rows, local_heads, head_size
    )


def per_device(frames, lengths, w_qkv, w_out, cotangent):
    width = w_out.shape[0]
    head_size = width // H
    scale = float(head_size) ** (-0.5)
    tok_rows = frames.shape[1]
    seq_count = lax.axis_size("seq")
    groups = max(1, seq_count // H)
    local_heads = max(1, H // seq_count)
    head_blocks = H // local_heads
    part_rows = tok_rows // groups
    frame_total = tok_rows * seq_count
    group_index = lax.axis_index("seq") % groups
    length = lengths[0]
    inputs = frames[0].astype(jnp.float32)
    normed = layer_norm(inputs).astype(jnp.bfloat16)
    qkv = jnp.dot(normed, w_qkv, preferred_element_type=jnp.float32).astype(jnp.bfloat16)
    qkv_local = qkv.reshape(tok_rows, 3, H, head_size)
    query_send = to_heads(qkv_local[:, 0], groups, head_blocks)
    paired = (
        qkv_local[:, 1:]
        .reshape(tok_rows, 2, head_blocks, local_heads, head_size)
        .transpose(2, 0, 1, 3, 4)
    )
    paired_send = jnp.broadcast_to(
        paired[:, None], (head_blocks, groups, tok_rows, 2, local_heads, head_size)
    )
    paired_send = paired_send.reshape(seq_count, tok_rows, 2, local_heads, head_size)
    query_recv, paired_recv = (
        lax.all_to_all(query_send, "seq", split_axis=0, concat_axis=0, tiled=True),
        lax.all_to_all(paired_send, "seq", split_axis=0, concat_axis=0, tiled=True),
    )
    queries = query_recv.reshape(seq_count * part_rows, local_heads, head_size)
    keys = paired_recv[:, :, 0].reshape(frame_total, local_heads, head_size)
    values = paired_recv[:, :, 1].reshape(frame_total, local_heads, head_size)
    position = jnp.arange(frame_total, dtype=jnp.int32)
    bias = jnp.where(position < length, 0.0, -1000000000.0).astype(jnp.float32)
    offset = lax.axis_index("seq") * tok_rows
    own_pos = offset + jnp.arange(tok_rows, dtype=jnp.int32)
    valid = (own_pos < length).astype(jnp.float32)
    query = qkv_local[:, 0]
    top = jnp.full((H, tok_rows), -1e30, jnp.float32)
    key_piece = lax.all_gather(qkv_local[:, 1], "seq", axis=0, tiled=True)
    value_piece = lax.all_gather(qkv_local[:, 2], "seq", axis=0, tiled=True)
    key_pos = jnp.arange(key_piece.shape[0], dtype=jnp.int32)
    key_bias = jnp.where(key_pos < length, 0.0, -1000000000.0).astype(jnp.float32)
    scores = (
        jnp.einsum("qhd,khd->hqk", query, key_piece, preferred_element_type=jnp.float32) * scale
    )
    scores = scores + key_bias[None, None, :]
    new_top = jnp.maximum(top, jnp.max(scores, axis=2))
    expo = jnp.exp(scores - new_top[:, :, None])
    total = jnp.sum(expo, axis=2)
    accum = jnp.einsum(
        "hqk,khd->hqd", expo.astype(jnp.bfloat16), value_piece, preferred_element_type=jnp.float32
    )
    top, total, accum = (new_top, total, accum)
    context = (
        (accum / total[:, :, None]).astype(jnp.bfloat16).transpose(1, 0, 2).reshape(tok_rows, width)
    )
    branch = jnp.dot(context, w_out, preferred_element_type=jnp.float32)
    output = (inputs + valid[:, None] * branch).astype(jnp.bfloat16)
    grad_rows = (cotangent[0].astype(jnp.float32) * valid[:, None]).astype(jnp.bfloat16)
    columns = context
    out_share = lax.psum_scatter(
        jnp.dot(columns.T, grad_rows, preferred_element_type=jnp.float32),
        "seq",
        scatter_dimension=0,
        tiled=True,
    )
    dcontext = jnp.dot(grad_rows, w_out.T, preferred_element_type=jnp.float32).astype(jnp.bfloat16)
    dcontext_send = to_heads(dcontext.reshape(tok_rows, H, head_size), groups, head_blocks)
    dcontext_heads = lax.all_to_all(dcontext_send, "seq", split_axis=0, concat_axis=0, tiled=True)
    dcontext_heads = dcontext_heads.reshape(seq_count * part_rows, local_heads, head_size)
    dquery, dkeys, dvalues = head_backward(
        queries[:, 0], keys[:, 0], values[:, 0], dcontext_heads[:, 0], bias, scale
    )
    query_grads = [dquery]
    paired_grads = [jnp.stack([dkeys, dvalues], axis=1)]
    query_block = jnp.stack(query_grads, axis=1).reshape(
        seq_count, part_rows, 1, local_heads, head_size
    )
    paired_block = jnp.stack(paired_grads, axis=2)
    split_grads = paired_block.reshape(seq_count, groups, part_rows, 2, local_heads, head_size)
    own_half = lax.dynamic_index_in_dim(split_grads, group_index, 1, keepdims=False)
    other_half = lax.dynamic_index_in_dim(split_grads, 1 - group_index, 1, keepdims=False)
    partner_half = from_partner(other_half, "seq", 0)
    paired_rows = (own_half + partner_half).astype(jnp.bfloat16)
    dtrio = jnp.concatenate([query_block, paired_rows], axis=2)
    returned_grads = lax.all_to_all(dtrio, "seq", split_axis=0, concat_axis=0, tiled=True)
    dqkv = returned_grads.reshape(head_blocks, groups, part_rows, 3, local_heads, head_size)
    dqkv = dqkv.transpose(1, 2, 3, 0, 4, 5).reshape(tok_rows, 3 * width)
    columns = normed
    qkv_share = lax.psum_scatter(
        jnp.dot(columns.T, dqkv, preferred_element_type=jnp.float32),
        "seq",
        scatter_dimension=0,
        tiled=True,
    )
    grad_qkv, grad_out = lax.psum((qkv_share, out_share), "batch")
    dnormed = jnp.dot(dqkv, w_qkv.T, preferred_element_type=jnp.float32)
    unused, pull = jax.vjp(layer_norm, inputs)
    grad_input = (cotangent[0].astype(jnp.float32) + pull(dnormed)[0]).astype(jnp.bfloat16)
    return (output[None], grad_input[None], grad_qkv, grad_out)


def solution(mesh):
    return jax.shard_map(
        per_device,
        mesh=mesh,
        in_specs=(P("batch", "seq", None), P("batch"), P(), P(), P("batch", "seq", None)),
        out_specs=(
            P("batch", "seq", None),
            P("batch", "seq", None),
            P("seq", None),
            P("seq", None),
        ),
        check_vma=False,
    )
```

profile of v0, /device:TPU:0, one launch (start us, length us, event | category | flops | bytes accessed | tf_op | source)
XLA Modules:
  0.0 485.5 jit_solution(13089522208990970412)
XLA Ops:
  10.3 4.4 fusion.38
  16.9 1.8 copy.43
  19.1 1.5 broadcast_in_dim.61
  20.6 8.0 %all-to-all-start.1 = ((bf16[16,192,2,1,128]{4,1,3,2,0:T(8,128)(2,1)}), bf16[16,192,2,1,128]{4,1,3,2,0:T(8,128)(2,1)}, u32[]{:S(2)}, u32[]{:S(2)}) async-start(bf16[16,192,2,1,128]{4,1,3,2,0:T(8,128)(2,1)} %bitcast.192), calls=%async_computation.1 | async-start | bytes 3145728 | tf_op jit(solution)/shard_map/all_to_all | solution.py:92
  32.0 26.6 %all-to-all-done.1 = bf16[16,192,2,1,128]{4,1,3,2,0:T(8,128)(2,1)} async-done(((bf16[16,192,2,1,128]{4,1,3,2,0:T(8,128)(2,1)}), bf16[16,192,2,1,128]{4,1,3,2,0:T(8,128)(2,1)}, u32[]{:S(2)}, u32[]{:S(2)}) %all-to-all-start.1) | async-done | bytes 1572896 | tf_op jit(solution)/shard_map/all_to_all | solution.py:92
  58.7 3.6 all-to-all-start
  62.2 2.4 fusion.103
  64.6 31.5 %all-gather.5.cloned.1.call-done = bf16[3072,1,8,128]{3,0,2,1:T(8,128)(2,1)} async-done(((bf16[192,1,8,128]{3,0,2,1:T(8,128)(2,1)}), bf16[3072,1,8,128]{3,0,2,1:T(8,128)(2,1)}) %all-gather.5.cloned.1.call-update) | async-done | bytes 6291472 | tf_op jit(solution)/shard_map/all_gather | solution.py:104
  96.1 12.2 %fusion.26 = (f32[8,192]{1,0:T(8,128)S(1)}, f32[8,192,3072]{2,1,0:T(8,128)}) fusion(f32[3072]{0:T(1024)S(1)} %fusion.98, bf16[3072,1,8,128]{3,0,2,1:T(8,128)(2,1)} %all-gather.5.cloned.1.call-done, bf16[192,1,8,128]{3,2,1,0:T(8,128)(2,1)} %get-tuple-element.117), kind=kOutput, calls=%fused_computation.34 | convolution fusion | flops 1222113792 | bytes 25577472 | tf_op jit(solution)/shard_map/qhd,khd->hqk/dot_general | solution.py:109
  108.3 10.3 %fusion.27 = f32[8,192]{1,0:T(8,128)S(1)} fusion(f32[8,192,3072]{2,1,0:T(8,128)} %get-tuple-element.121, f32[8,192]{1,0:T(8,128)S(1)} %broadcast_maximum_fusion, f32[3072]{0:T(1024)S(1)} %fusion.98), kind=kLoop, calls=%fused_computation.35 | loop fusion | flops 18872832 | bytes 18898944 | tf_op jit(solution)/shard_map/reduce_sum | solution.py:114
  118.6 4.5 all-to-all-start.2
  123.4 35.3 %all-gather.7.cloned.1.call-done = bf16[3072,1,8,128]{3,0,2,1:T(8,128)(2,1)} async-done(((bf16[192,1,8,128]{3,0,2,1:T(8,128)(2,1)}), bf16[3072,1,8,128]{3,0,2,1:T(8,128)(2,1)}) %all-gather.7.cloned.1.call-update) | async-done | bytes 6291472 | tf_op jit(solution)/shard_map/all_gather | solution.py:105
  158.7 10.5 %fusion.65 = bf16[8,24,8,128]{3,2,1,0:T(8,128)(2,1)S(1)} fusion(bf16[3072,1,8,128]{3,0,2,1:T(8,128)(2,1)} %all-gather.7.cloned.1.call-done, f32[8,192,3072]{2,1,0:T(8,128)} %get-tuple-element.121, f32[8,192]{1,0:T(8,128)S(1)} %broadcast_maximum_fusion, f32[3072]{0:T(1024)S(1)} %fusion.98, f32[192,8]{0,1:T(8,128)S(1)} %bitcast.199), kind=kOutput, calls=%fused_computation.76 | convolution fusion | flops 1227227136 | bytes 25583616 | tf_op jit(solution)/shard_map/hqk,khd->hqd/dot_general | solution.py:115
  169.9 2.7 fusion.83
  172.8 68.9 %while.15 = (s32[]{:T(128)}, f32[3072,128]{1,0:T(8,128)}, f32[3072,128]{1,0:T(8,128)}, bf16[3,512,128]{2,1,0:T(8,128)(2,1)}, bf16[3,512,128]{2,1,0:T(8,128)(2,1)...) while((s32[]{:T(128)}, f32[3072,128]{1,0:T(8,128)}, ...), condition=%wide.region_8.9_spmd.clone, body=%wide.region_4.0_spmd.clone.sunk | while | flops 2054689280 | bytes 116358872 | solution.py:49
  174.5 2.7 copy-done.1
  177.2 1.4 fusion.139
  178.6 5.8 %convolution_add_fusion.2 = f32[3072,128]{1,0:T(8,128)} fusion(f32[3072,128]{1,0:T(8,128)} %get-tuple-element.200, pred[]{:T(512)S(6)} %compare.4, bf16[3,512,128]{2,1,0:T(8,128)(2,1)} %get-tuple-element.215, s32[]{:T(128)} %get-tuple-element.198, f32[512,3072]{1,0:T(8,128)} %copy-done.1, f32[512]{0:T(512)S(1)} %fusion.139, ...), kind=kOutput, calls=%fused_computation.8.clone.1 | convolution fusion | flops 411303936 | bytes 9585153 | tf_op jit(solution)/shard_map/while/body/eval_jaxpr/dot_general | solution.py:45
  184.4 3.2 multiply_reduce_fusion.2
  187.6 2.9 multiply_convert_fusion.2
  190.6 2.2 fusion.140
  192.8 1.6 fusion.141
  196.2 2.7 copy-done.1
  198.8 1.4 fusion.139
  200.2 6.4 %convolution_add_fusion.2 = f32[3072,128]{1,0:T(8,128)} fusion(f32[3072,128]{1,0:T(8,128)} %get-tuple-element.200, pred[]{:T(512)S(6)} %compare.4, bf16[3,512,128]{2,1,0:T(8,128)(2,1)} %get-tuple-element.215, s32[]{:T(128)} %get-tuple-element.198, f32[512,3072]{1,0:T(8,128)} %copy-done.1, f32[512]{0:T(512)S(1)} %fusion.139, ...), kind=kOutput, calls=%fused_computation.8.clone.1 | convolution fusion | flops 411303936 | bytes 9585153 | tf_op jit(solution)/shard_map/while/body/eval_jaxpr/dot_general | solution.py:45
  206.6 3.2 multiply_reduce_fusion.2
  209.8 2.9 multiply_convert_fusion.2
  212.8 3.6 fusion.140
  216.4 1.6 fusion.141
  219.7 2.7 copy-done.1
  223.8 6.4 %convolution_add_fusion.2 = f32[3072,128]{1,0:T(8,128)} fusion(f32[3072,128]{1,0:T(8,128)} %get-tuple-element.200, pred[]{:T(512)S(6)} %compare.4, bf16[3,512,128]{2,1,0:T(8,128)(2,1)} %get-tuple-element.215, s32[]{:T(128)} %get-tuple-element.198, f32[512,3072]{1,0:T(8,128)} %copy-done.1, f32[512]{0:T(512)S(1)} %fusion.139, ...), kind=kOutput, calls=%fused_computation.8.clone.1 | convolution fusion | flops 411303936 | bytes 9585153 | tf_op jit(solution)/shard_map/while/body/eval_jaxpr/dot_general | solution.py:45
  230.2 3.2 multiply_reduce_fusion.2
  233.4 2.9 multiply_convert_fusion.2
  236.3 3.7 fusion.140
  240.0 1.6 fusion.141
  241.7 2.1 fusion.35
  243.9 1.5 collective-permute-start
  245.4 35.8 %collective-permute-done = f32[16,96,2,1,128]{4,1,3,2,0:T(8,128)S(1)} collective-permute-done((f32[16,96,2,1,128]{4,1,3,2,0:T(8,128)S(1)}, f32[16,96,2,1,128]{4,1,3,2,0:T(8,128)S(1)}, u32[]{:S(2)}, u32[]{:S(2)}) %collective-permute-start) | collective-permute-done | bytes 1572896 | tf_op jit(solution)/shard_map/ppermute | solution.py:10
  282.6 22.8 %all_to_all.20 = bf16[16,96,3,1,128]{4,1,3,2,0:T(8,128)(2,1)S(1)} all-to-all(bf16[16,96,3,1,128]{4,1,3,2,0:T(8,128)(2,1)S(1)} %pad_maximum_fusion), channel_id=1, replica_groups=mesh['batch'=8,'seq'=16] {'seq'}, dimensions={0} | all-to-all | bytes 2359296 | tf_op jit(solution)/shard_map/all_to_all | solution.py:151
  305.5 1.8 copy.39
  307.3 3.0 reshape.115
  310.3 7.7 %fusion.79 = f32[1024,3072]{1,0:T(8,128)} fusion(bf16[192,3072]{1,0:T(8,128)(2,1)} %reshape.115, bf16[1,192,1024]{2,1,0:T(8,128)(2,1)S(1)} %copy-done.3, f32[192]{0:T(256)S(1)} %copy-done.15, f32[192]{0:T(256)S(1)} %copy-done.13), kind=kOutput, calls=%fused_computation.87 | convolution fusion | flops 1208745984 | bytes 14157312 | tf_op jit(solution)/shard_map/dot_general | solution.py:156
  318.1 5.5 %fusion.75 = (f32[192]{0:T(256)S(1)}, f32[192,1024]{1,0:T(8,128)S(1)}) fusion(bf16[1,192,1024]{2,1,0:T(8,128)(2,1)S(1)} %copy-done.3, f32[192]{0:T(256)S(1)} %copy-done.13, bf16[192,3072]{1,0:T(8,128)(2,1)} %reshape.115, bf16[1024,3072]{1,0:T(8,128)(2,1)} %param.9), kind=kOutput, calls=%fused_computation.82 | convolution fusion | flops 1208745728 | bytes 8652288 | tf_op jit(solution)/shard_map/dot_general | solution.py:162
  324.9 86.4 %reduce-scatter.3.cloned.1.call-done = f32[64,3072]{1,0:T(8,128)} async-done(((f32[1024,3072]{1,0:T(8,128)}), f32[64,3072]{1,0:T(8,128)}) %reduce-scatter.3.cloned.1.call-update) | async-done | bytes 786448 | tf_op jit(solution)/shard_map/reduce_scatter | solution.py:155
  411.3 2.2 fusion.85
  414.9 60.3 %all-reduce.3.cloned.1.call-done = (f32[64,3072]{1,0:T(8,128)}, f32[64,1024]{1,0:T(8,128)}) async-done(((f32[64,3072]{1,0:T(8,128)}, f32[64,1024]{1,0:T(8,128)}), (f32[64,3072]{1,0:T(8,128)}, f32[64,1024]{1,0:T(8,128)})) %all-reduce.3.cloned.1.call-update) | async-done | bytes 1048592 | tf_op jit(solution)/shard_map/psum | solution.py:161
  475.2 2.1 copy.86
  477.3 1.7 copy.87
  (95 shorter events, 20.0 us)
Async XLA Ops:
  7.2 23.1 %copy-start = (bf16[1024,1024]{1,0:T(8,128)(2,1)S(1)}, bf16[1024,1024]{1,0:T(8,128)(2,1)}, u32[]{:S(2)}) copy-start(bf16[1024,1024]{1,0:T(8,128)(2,1)} %param.10) | copy-start | bytes 6291460
  7.2 89.0 %all-gather.5.cloned.1.call-start = ((), (), s32[]{:S(2)}) async-start(), calls=%async_computation.8 | async-start | bytes 6684672 | tf_op jit(solution)/shard_map/all_gather | solution.py:104
  8.5 6.2 %copy-start.12 = (f32[192]{0:T(256)}, f32[192]{0:T(256)S(1)}, u32[]{:S(2)}) copy-start(f32[192]{0:T(256)S(1)} %broadcast_multiply_fusion) | copy-start | bytes 2308
  9.8 0.5 copy-start.16
  10.3 4.4 copy-start.14
  16.9 141.8 %all-gather.7.cloned.1.call-start = ((), (), s32[]{:S(2)}) async-start(), calls=%async_computation.9 | async-start | bytes 6684672 | tf_op jit(solution)/shard_map/all_gather | solution.py:105
  18.9 9.8 %copy-start.4 = (bf16[192,1,8,128]{3,2,1,0:T(8,128)(2,1)S(1)}, bf16[192,1,8,128]{3,2,1,0:T(8,128)(2,1)}, u32[]{:S(2)}) copy-start(bf16[192,1,8,128]{3,2,1,0:T(8,128)(2,1)} %get-tuple-element.117) | copy-start | bytes 1179652
  18.9 11.3 %copy-start.5 = (bf16[1,192,1024]{2,1,0:T(8,128)(2,1)S(1)}, bf16[1,192,1024]{2,1,0:T(8,128)(2,1)}, u32[]{:S(2)}) copy-start(bf16[1,192,1024]{2,1,0:T(8,128)(2,1)} %param.11) | copy-start | bytes 1179652
  20.6 38.0 %all-to-all-start.1 = ((bf16[16,192,2,1,128]{4,1,3,2,0:T(8,128)(2,1)}), bf16[16,192,2,1,128]{4,1,3,2,0:T(8,128)(2,1)}, u32[]{:S(2)}, u32[]{:S(2)}) async-start(bf16[16,192,2,1,128]{4,1,3,2,0:T(8,128)(2,1)} %bitcast.192), calls=%async_computation.1 | async-start | bytes 3145728 | tf_op jit(solution)/shard_map/all_to_all | solution.py:92
  30.2 138.9 %copy-start.18 = (f32[192]{0:T(256)}, f32[192]{0:T(256)S(1)}, u32[]{:S(2)}) copy-start(f32[192]{0:T(256)S(1)} %compare_convert_fusion) | copy-start | bytes 2308
  58.7 59.9 %all-to-all-start = ((bf16[16,96,1,128]{3,1,2,0:T(8,128)(2,1)}), bf16[16,96,1,128]{3,1,2,0:T(8,128)(2,1)S(1)}, u32[]{:S(2)}, u32[]{:S(2)}) async-start(bf16[16,96,1,128]{3,1,2,0:T(8,128)(2,1)} %bitcast.11), calls=%async_computation | async-start | bytes 786432 | tf_op jit(solution)/shard_map/all_to_all | solution.py:91
  118.6 54.2 %all-to-all-start.2 = ((bf16[16,96,1,128]{3,1,2,0:T(8,128)(2,1)}), bf16[16,96,1,128]{3,1,2,0:T(8,128)(2,1)}, u32[]{:S(2)}, u32[]{:S(2)}) async-start(bf16[16,96,1,128]{3,1,2,0:T(8,128)(2,1)} %bitcast.195), calls=%async_computation.2 | async-start | bytes 786432 | tf_op jit(solution)/shard_map/all_to_all | solution.py:134
  123.1 201.8 %reduce-scatter.5.cloned.1.call-start = ((), (), s32[]{:S(2)}) async-start(), calls=%async_computation.7 | async-start | bytes 4456448 | tf_op jit(solution)/shard_map/reduce_scatter | solution.py:126
  158.7 11.3 %copy-start.6 = (bf16[1,192,1024]{2,1,0:T(8,128)(2,1)S(1)}, bf16[1,192,1024]{2,1,0:T(8,128)(2,1)}, u32[]{:S(2)}) copy-start(bf16[1,192,1024]{2,1,0:T(8,128)(2,1)} %param.11) | copy-start | bytes 1179652
  169.2 0.7 copy-start.10
  172.7 238.6 %reduce-scatter.3.cloned.1.call-start = ((), (), s32[]{:S(2)}) async-start(), calls=%async_computation.6 | async-start | bytes 13369344 | tf_op jit(solution)/shard_map/reduce_scatter | solution.py:155
  174.5 2.7 copy-start.1
  178.5 5.9 %copy-start.2 = (f32[512,3072]{1,0:T(8,128)S(1)}, f32[512,3072]{1,0:T(8,128)}, u32[]{:S(2)}) copy-start(f32[512,3072]{1,0:T(8,128)} %copy-done.1) | copy-start | bytes 18874372 | tf_op jit(solution)/shard_map/while
  178.6 5.9 %copy-start.9 = (bf16[3072,128]{1,0:T(8,128)(2,1)S(1)}, bf16[3072,128]{1,0:T(8,128)(2,1)}, u32[]{:S(2)}) copy-start(bf16[3072,128]{1,0:T(8,128)(2,1)} %get-tuple-element.216) | copy-start | bytes 2359300 | tf_op jit(solution)/shard_map/while
  196.1 2.7 copy-start.1
  200.2 6.4 %copy-start.2 = (f32[512,3072]{1,0:T(8,128)S(1)}, f32[512,3072]{1,0:T(8,128)}, u32[]{:S(2)}) copy-start(f32[512,3072]{1,0:T(8,128)} %copy-done.1) | copy-start | bytes 18874372 | tf_op jit(solution)/shard_map/while
  200.2 6.4 %copy-start.9 = (bf16[3072,128]{1,0:T(8,128)(2,1)S(1)}, bf16[3072,128]{1,0:T(8,128)(2,1)}, u32[]{:S(2)}) copy-start(bf16[3072,128]{1,0:T(8,128)(2,1)} %get-tuple-element.216) | copy-start | bytes 2359300 | tf_op jit(solution)/shard_map/while
  219.7 2.7 copy-start.1
  223.8 6.4 %copy-start.2 = (f32[512,3072]{1,0:T(8,128)S(1)}, f32[512,3072]{1,0:T(8,128)}, u32[]{:S(2)}) copy-start(f32[512,3072]{1,0:T(8,128)} %copy-done.1) | copy-start | bytes 18874372 | tf_op jit(solution)/shard_map/while
  223.8 6.4 %copy-start.9 = (bf16[3072,128]{1,0:T(8,128)(2,1)S(1)}, bf16[3072,128]{1,0:T(8,128)(2,1)}, u32[]{:S(2)}) copy-start(bf16[3072,128]{1,0:T(8,128)(2,1)} %get-tuple-element.216) | copy-start | bytes 2359300 | tf_op jit(solution)/shard_map/while
  243.9 37.4 %collective-permute-start = (f32[16,96,2,1,128]{4,1,3,2,0:T(8,128)S(1)}, f32[16,96,2,1,128]{4,1,3,2,0:T(8,128)S(1)}, u32[]{:S(2)}, u32[]{:S(2)}) collective-permute-start(f32[16,96,2,1,128]{4,1,3,2,0:T(8,128)S(1)} %bitcast.194), channel_id=1, source_target_pairs={{0,1},{1,0},{2,3},{3,2},{4,5},{5,4},{6,7},{7,6},{8,9},{9,8},{10,11... | collective-permute-start | bytes 4718600 | tf_op jit(solution)/shard_map/ppermute | solution.py:10
  281.3 29.0 %copy-start.3 = (bf16[1,192,1024]{2,1,0:T(8,128)(2,1)S(1)}, bf16[1,192,1024]{2,1,0:T(8,128)(2,1)}, u32[]{:S(2)}) copy-start(bf16[1,192,1024]{2,1,0:T(8,128)(2,1)} %param.7) | copy-start | bytes 1179652
  281.3 29.0 %copy-start.13 = (f32[192]{0:T(256)S(1)}, f32[192]{0:T(256)}, u32[]{:S(2)}) copy-start(f32[192]{0:T(256)} %copy-done.12) | copy-start | bytes 2308
  281.3 29.0 %copy-start.15 = (f32[192]{0:T(256)S(1)}, f32[192]{0:T(256)}, u32[]{:S(2)}) copy-start(f32[192]{0:T(256)} %copy-done.14) | copy-start | bytes 2308
  318.0 5.6 %copy-start.17 = (f32[192]{0:T(256)S(1)}, f32[192]{0:T(256)}, u32[]{:S(2)}) copy-start(f32[192]{0:T(256)} %copy-done.16) | copy-start | bytes 2308
  318.1 93.3 %copy-start.7 = (bf16[1,192,1024]{2,1,0:T(8,128)(2,1)S(1)}, bf16[1,192,1024]{2,1,0:T(8,128)(2,1)}, u32[]{:S(2)}) copy-start(bf16[1,192,1024]{2,1,0:T(8,128)(2,1)} %param.11) | copy-start | bytes 1179652
  318.1 95.5 %copy-start.11 = (bf16[8,24,8,128]{3,2,1,0:T(8,128)(2,1)S(1)}, bf16[8,24,8,128]{3,2,1,0:T(8,128)(2,1)}, u32[]{:S(2)}) copy-start(bf16[8,24,8,128]{3,2,1,0:T(8,128)(2,1)} %copy-done.10) | copy-start | bytes 1179652
  318.1 95.5 %copy-start.19 = (f32[192]{0:T(256)S(1)}, f32[192]{0:T(256)}, u32[]{:S(2)}) copy-start(f32[192]{0:T(256)} %copy-done.18) | copy-start | bytes 2308
  318.1 157.1 %all-reduce.3.cloned.1.call-start = ((), (), s32[]{:S(2)}) async-start(), calls=%async_computation.10 | async-start | bytes 2097152 | tf_op jit(solution)/shard_map/psum | solution.py:161
  323.7 0.9 copy-start.8
Sparse Core Ops, SparseCore 0:
  17.0 79.0 all-gather.4
  98.3 60.3 all-gather.6
  172.8 77.9 reduce-scatter.4
  318.2 93.0 reduce-scatter.2
  413.6 61.5 all-reduce.2
where the time goes:
time: 487 us; the launch traced here: 485 us
  waiting for transfers between devices  276 us (57%)
  matrix products  91.2 us (19%)
  other arithmetic  33.6 us (7%)
  local copies, waits for them, and re-layouts  28.7 us (6%)
  blocking collectives  22.8 us (5%)
  starting transfers between devices  18 us (4%)
  between operations  14.8 us (3%)
    reduce_scatter x1, waiting for transfers between devices, per_device(): lax.psum_scatter(jnp.dot(columns.T, dqkv, preferred_element_type=jnp.floa...  86.4 us
    psum x1, waiting for transfers between devices, per_device(): grad_qkv, grad_out = lax.psum((qkv_share, out_share), 'batch')  60.3 us
    ppermute x1, waiting for transfers between devices, from_partner(): lax.ppermute(array, axis, [(i, i ^ 1 << stride) for i in range(lax.axis_s...  35.8 us
    all_gather x1, waiting for transfers between devices, per_device(): value_piece = lax.all_gather(qkv_local[:, 2], 'seq', axis=0, tiled=True)  35.3 us
    all_gather x1, waiting for transfers between devices, per_device(): key_piece = lax.all_gather(qkv_local[:, 1], 'seq', axis=0, tiled=True)  31.5 us
    all_to_all x1, waiting for transfers between devices, per_device(): lax.all_to_all(paired_send, 'seq', split_axis=0, concat_axis=0, tiled=True)  26.6 us
    all_to_all x1, blocking collectives, per_device(): lax.all_to_all(dtrio, 'seq', split_axis=0, concat_axis=0, tiled=True)  22.8 us
    dot_general x3, matrix products, step(): jnp.dot(p_half.T, d_rows, preferred_element_type=jnp.float32)  18.6 us
  transfers between devices with their start and end apart: 9, of which 6 were waited for; matrix products, arithmetic and copies ran while one was open for 27% of the time, Pallas kernels for 0%

commit v1 on v0

--- a/solution.py
+++ b/solution.py
@@ -4,6 +4,11 @@
 from jax.sharding import PartitionSpec as P
 
 H = 8
+
+
+def exchange_gather(x, mesh_axis, dim):
+    repeated = jnp.stack([x] * lax.axis_size(mesh_axis))
+    return jnp.concatenate(lax.all_to_all(repeated, mesh_axis, 0, 0), axis=dim)
 
 
 def from_partner(array, axis, stride):
@@ -101,7 +106,7 @@
     valid = (own_pos < length).astype(jnp.float32)
     query = qkv_local[:, 0]
     top = jnp.full((H, tok_rows), -1e30, jnp.float32)
-    key_piece = lax.all_gather(qkv_local[:, 1], "seq", axis=0, tiled=True)
+    key_piece = exchange_gather(qkv_local[:, 1], "seq", 0)
     value_piece = lax.all_gather(qkv_local[:, 2], "seq", axis=0, tiled=True)
     key_pos = jnp.arange(key_piece.shape[0], dtype=jnp.int32)
     key_bias = jnp.where(key_pos < length, 0.0, -1000000000.0).astype(jnp.float32)

time: 487 us -> 539 us (1.11)
  waiting for transfers between devices: 276 us -> 315 us
  starting transfers between devices: 18 us -> 30.2 us
  local copies, waits for them, and re-layouts: 28.7 us -> 34.7 us
    all_to_all x0 -> x1, waiting for transfers between devices: none -> 102 us  [exchange_gather(): return jnp.concatenate(lax.all_to_all(repeated, mesh_axis, 0, 0), axis=dim)]
    all_gather x1, waiting for transfers between devices: 35.3 us -> 0.02 us  [per_device(): value_piece = lax.all_gather(qkv_local[:, 2], 'seq', axis=0, tiled=True)]
    all_gather x1 -> x0, waiting for transfers between devices: 31.5 us -> none  [per_device(): key_piece = lax.all_gather(qkv_local[:, 1], 'seq', axis=0, tiled=True)]
  transfers between devices with their start and end apart: 9 -> 9, of which waited for: 6 -> 5; matrix products, arithmetic and copies ran while one was open for 27% -> 25% of each run, Pallas kernels for 0% -> 0%
where the time goes in v1:
time: 539 us; the launch traced here: 538 us
  waiting for transfers between devices  315 us (58%)
  matrix products  87 us (16%)
  local copies, waits for them, and re-layouts  34.7 us (6%)
  other arithmetic  33.4 us (6%)
  starting transfers between devices  30.2 us (6%)
  blocking collectives  22.8 us (4%)
  between operations  14.8 us (3%)
    all_to_all x1, waiting for transfers between devices, exchange_gather(): return jnp.concatenate(lax.all_to_all(repeated, mesh_axis, 0, 0), axis=dim)  102 us
    reduce_scatter x1, waiting for transfers between devices, per_device(): lax.psum_scatter(jnp.dot(columns.T, dqkv, preferred_element_type=jnp.floa...  87.8 us
    psum x1, waiting for transfers between devices, per_device(): grad_qkv, grad_out = lax.psum((qkv_share, out_share), 'batch')  60.3 us
    ppermute x1, waiting for transfers between devices, from_partner(): lax.ppermute(array, axis, [(i, i ^ 1 << stride) for i in range(lax.axis_s...  34.8 us
    all_to_all x1, waiting for transfers between devices, per_device(): lax.all_to_all(paired_send, 'seq', split_axis=0, concat_axis=0, tiled=True)  29.6 us
    all_to_all x1, blocking collectives, per_device(): lax.all_to_all(dtrio, 'seq', split_axis=0, concat_axis=0, tiled=True)  22.8 us
    dot_general x3, matrix products, step(): jnp.dot(p_half.T, d_rows, preferred_element_type=jnp.float32)  18.6 us
  transfers between devices with their start and end apart: 9, of which 5 were waited for; matrix products, arithmetic and copies ran while one was open for 25% of the time, Pallas kernels for 0%

profile of v1, /device:TPU:0, one launch (start us, length us, event | category | flops | bytes accessed | tf_op | source)
XLA Modules:
  0.0 537.8 jit_solution(10099832365569063754)
XLA Ops:
  10.3 4.4 fusion.36
  17.3 1.5 broadcast_in_dim.61
  18.8 8.0 %all-to-all-start.2 = ((bf16[16,192,2,1,128]{4,1,3,2,0:T(8,128)(2,1)}), bf16[16,192,2,1,128]{4,1,3,2,0:T(8,128)(2,1)}, u32[]{:S(2)}, u32[]{:S(2)}) async-start(bf16[16,192,2,1,128]{4,1,3,2,0:T(8,128)(2,1)} %bitcast.192), calls=%async_computation.2 | async-start | bytes 3145728 | tf_op jit(solution)/shard_map/all_to_all | solution.py:97
  26.9 29.6 %all-to-all-done.2 = bf16[16,192,2,1,128]{4,1,3,2,0:T(8,128)(2,1)} async-done(((bf16[16,192,2,1,128]{4,1,3,2,0:T(8,128)(2,1)}), bf16[16,192,2,1,128]{4,1,3,2,0:T(8,128)(2,1)}, u32[]{:S(2)}, u32[]{:S(2)}) %all-to-all-start.2) | async-done | bytes 1572896 | tf_op jit(solution)/shard_map/all_to_all | solution.py:97
  56.5 4.3 stack.12
  60.7 4.8 all-to-all-start
  68.9 2.4 fusion.102
  71.2 102.1 %all-to-all-done = bf16[16,192,8,128]{3,1,2,0:T(8,128)(2,1)} async-done(((bf16[16,192,8,128]{3,1,2,0:T(8,128)(2,1)}), bf16[16,192,8,128]{3,1,2,0:T(8,128)(2,1)}, u32[]{:S(2)}, u32[]{:S(2)}) %all-to-all-start) | async-done | bytes 6291488 | tf_op jit(solution)/shard_map/all_to_all | solution.py:11
  173.3 7.5 %all-to-all-start.1 = ((bf16[16,96,1,128]{3,1,2,0:T(8,128)(2,1)}), bf16[16,96,1,128]{3,1,2,0:T(8,128)(2,1)S(1)}, u32[]{:S(2)}, u32[]{:S(2)}) async-start(bf16[16,96,1,128]{3,1,2,0:T(8,128)(2,1)} %bitcast.196), calls=%async_computation.1 | async-start | bytes 786432 | tf_op jit(solution)/shard_map/all_to_all | solution.py:96
  180.8 3.4 copy.32
  184.3 7.9 %fusion.26 = (f32[8,192]{1,0:T(8,128)S(1)}, f32[8,192,3072]{2,1,0:T(8,128)}) fusion(f32[3072]{0:T(1024)S(1)} %fusion.97, bf16[3072,8,128]{2,0,1:T(8,128)(2,1)S(1)} %bitcast.187, bf16[192,1,8,128]{3,2,1,0:T(8,128)(2,1)S(1)} %copy-done.5), kind=kOutput, calls=%fused_computation.34 | convolution fusion | flops 1222113792 | bytes 25577472 | tf_op jit(solution)/shard_map/qhd,khd->hqk/dot_general | solution.py:114
  192.2 10.2 %fusion.27 = f32[8,192]{1,0:T(8,128)S(1)} fusion(f32[8,192,3072]{2,1,0:T(8,128)} %get-tuple-element.121, f32[8,192]{1,0:T(8,128)S(1)} %broadcast_maximum_fusion, f32[3072]{0:T(1024)S(1)} %fusion.97), kind=kLoop, calls=%fused_computation.35 | loop fusion | flops 18872832 | bytes 18898944 | tf_op jit(solution)/shard_map/reduce_sum | solution.py:119
  202.3 7.3 %all-to-all-start.3 = ((bf16[16,96,1,128]{3,1,2,0:T(8,128)(2,1)}), bf16[16,96,1,128]{3,1,2,0:T(8,128)(2,1)}, u32[]{:S(2)}, u32[]{:S(2)}) async-start(bf16[16,96,1,128]{3,1,2,0:T(8,128)(2,1)} %bitcast.195), calls=%async_computation.3 | async-start | bytes 786432 | tf_op jit(solution)/shard_map/all_to_all | solution.py:139
  209.9 10.5 %fusion.63 = bf16[8,24,8,128]{3,2,1,0:T(8,128)(2,1)S(1)} fusion(bf16[3072,1,8,128]{3,0,2,1:T(8,128)(2,1)} %all-gather.3.cloned.1.call-done, f32[8,192,3072]{2,1,0:T(8,128)} %get-tuple-element.121, f32[8,192]{1,0:T(8,128)S(1)} %broadcast_maximum_fusion, f32[3072]{0:T(1024)S(1)} %fusion.97, f32[192,8]{0,1:T(8,128)S(1)} %bitcast.200), kind=kOutput, calls=%fused_computation.74 | convolution fusion | flops 1227227136 | bytes 25583616 | tf_op jit(solution)/shard_map/hqk,khd->hqd/dot_general | solution.py:120
  221.2 2.7 fusion.81
  224.0 69.0 %while.15 = (s32[]{:T(128)}, f32[3072,128]{1,0:T(8,128)}, f32[3072,128]{1,0:T(8,128)}, bf16[3,512,128]{2,1,0:T(8,128)(2,1)}, bf16[3,512,128]{2,1,0:T(8,128)(2,1)...) while((s32[]{:T(128)}, f32[3072,128]{1,0:T(8,128)}, ...), condition=%wide.region_8.9_spmd.clone, body=%wide.region_4.0_spmd.clone.sunk | while | flops 2054689280 | bytes 116358872 | solution.py:54
  225.7 2.7 copy-done.1
  229.8 5.9 %convolution_add_fusion.2 = f32[3072,128]{1,0:T(8,128)} fusion(f32[3072,128]{1,0:T(8,128)} %get-tuple-element.200, pred[]{:T(512)S(6)} %compare.4, bf16[3,512,128]{2,1,0:T(8,128)(2,1)} %get-tuple-element.215, s32[]{:T(128)} %get-tuple-element.198, f32[512,3072]{1,0:T(8,128)} %copy-done.1, f32[512]{0:T(512)S(1)} %fusion.139, ...), kind=kOutput, calls=%fused_computation.8.clone.1 | convolution fusion | flops 411303936 | bytes 9585153 | tf_op jit(solution)/shard_map/while/body/eval_jaxpr/dot_general | solution.py:50
  235.6 3.2 multiply_reduce_fusion.2
  238.9 2.9 multiply_convert_fusion.2
  241.8 2.3 fusion.140
  244.1 1.6 fusion.141
  247.4 2.7 copy-done.1
  251.5 6.3 %convolution_add_fusion.2 = f32[3072,128]{1,0:T(8,128)} fusion(f32[3072,128]{1,0:T(8,128)} %get-tuple-element.200, pred[]{:T(512)S(6)} %compare.4, bf16[3,512,128]{2,1,0:T(8,128)(2,1)} %get-tuple-element.215, s32[]{:T(128)} %get-tuple-element.198, f32[512,3072]{1,0:T(8,128)} %copy-done.1, f32[512]{0:T(512)S(1)} %fusion.139, ...), kind=kOutput, calls=%fused_computation.8.clone.1 | convolution fusion | flops 411303936 | bytes 9585153 | tf_op jit(solution)/shard_map/while/body/eval_jaxpr/dot_general | solution.py:50
  257.8 3.2 multiply_reduce_fusion.2
  261.1 2.9 multiply_convert_fusion.2
  264.0 3.7 fusion.140
  267.7 1.6 fusion.141
  271.0 2.7 copy-done.1
  273.7 1.4 fusion.139
  275.1 6.4 %convolution_add_fusion.2 = f32[3072,128]{1,0:T(8,128)} fusion(f32[3072,128]{1,0:T(8,128)} %get-tuple-element.200, pred[]{:T(512)S(6)} %compare.4, bf16[3,512,128]{2,1,0:T(8,128)(2,1)} %get-tuple-element.215, s32[]{:T(128)} %get-tuple-element.198, f32[512,3072]{1,0:T(8,128)} %copy-done.1, f32[512]{0:T(512)S(1)} %fusion.139, ...), kind=kOutput, calls=%fused_computation.8.clone.1 | convolution fusion | flops 411303936 | bytes 9585153 | tf_op jit(solution)/shard_map/while/body/eval_jaxpr/dot_general | solution.py:50
  281.5 3.2 multiply_reduce_fusion.2
  284.7 2.9 multiply_convert_fusion.2
  287.6 3.7 fusion.140
  291.3 1.6 fusion.141
  293.0 2.1 fusion.33
  295.1 2.3 collective-permute-start
  297.4 34.8 %collective-permute-done = f32[16,96,2,1,128]{4,1,3,2,0:T(8,128)S(1)} collective-permute-done((f32[16,96,2,1,128]{4,1,3,2,0:T(8,128)S(1)}, f32[16,96,2,1,128]{4,1,3,2,0:T(8,128)S(1)}, u32[]{:S(2)}, u32[]{:S(2)}) %collective-permute-start) | collective-permute-done | bytes 1572896 | tf_op jit(solution)/shard_map/ppermute | solution.py:15
  333.6 22.8 %all_to_all.25 = bf16[16,96,3,1,128]{4,1,3,2,0:T(8,128)(2,1)S(1)} all-to-all(bf16[16,96,3,1,128]{4,1,3,2,0:T(8,128)(2,1)S(1)} %pad_maximum_fusion), channel_id=1, replica_groups=mesh['batch'=8,'seq'=16] {'seq'}, dimensions={0} | all-to-all | bytes 2359296 | tf_op jit(solution)/shard_map/all_to_all | solution.py:156
  356.4 1.8 copy.40
  358.2 3.0 reshape.121
  361.2 7.7 %fusion.77 = f32[1024,3072]{1,0:T(8,128)} fusion(bf16[192,3072]{1,0:T(8,128)(2,1)} %reshape.121, bf16[1,192,1024]{2,1,0:T(8,128)(2,1)S(1)} %copy-done.3, f32[192]{0:T(256)S(1)} %copy-done.17, f32[192]{0:T(256)S(1)} %copy-done.15), kind=kOutput, calls=%fused_computation.85 | convolution fusion | flops 1208745984 | bytes 14157312 | tf_op jit(solution)/shard_map/dot_general | solution.py:161
  369.1 5.5 %fusion.73 = (f32[192]{0:T(256)S(1)}, f32[192,1024]{1,0:T(8,128)S(1)}) fusion(bf16[1,192,1024]{2,1,0:T(8,128)(2,1)S(1)} %copy-done.3, f32[192]{0:T(256)S(1)} %copy-done.15, bf16[192,3072]{1,0:T(8,128)(2,1)} %reshape.121, bf16[1024,3072]{1,0:T(8,128)(2,1)} %param.9), kind=kOutput, calls=%fused_computation.80 | convolution fusion | flops 1208745728 | bytes 8652288 | tf_op jit(solution)/shard_map/dot_general | solution.py:167
  375.8 87.8 %reduce-scatter.3.cloned.1.call-done = f32[64,3072]{1,0:T(8,128)} async-done(((f32[1024,3072]{1,0:T(8,128)}), f32[64,3072]{1,0:T(8,128)}) %reduce-scatter.3.cloned.1.call-update) | async-done | bytes 786448 | tf_op jit(solution)/shard_map/reduce_scatter | solution.py:160
  463.7 2.2 fusion.83
  467.2 60.3 %all-reduce.3.cloned.1.call-done = (f32[64,3072]{1,0:T(8,128)}, f32[64,1024]{1,0:T(8,128)}) async-done(((f32[64,3072]{1,0:T(8,128)}, f32[64,1024]{1,0:T(8,128)}), (f32[64,3072]{1,0:T(8,128)}, f32[64,1024]{1,0:T(8,128)})) %all-reduce.3.cloned.1.call-update) | async-done | bytes 1048592 | tf_op jit(solution)/shard_map/psum | solution.py:166
  527.6 2.1 copy.86
  529.6 1.7 copy.87
  (100 shorter events, 21.4 us)
Async XLA Ops:
  7.2 59.9 %copy-start = (bf16[1024,1024]{1,0:T(8,128)(2,1)S(1)}, bf16[1024,1024]{1,0:T(8,128)(2,1)}, u32[]{:S(2)}) copy-start(bf16[1024,1024]{1,0:T(8,128)(2,1)} %param.10) | copy-start | bytes 6291460
  7.2 202.7 %all-gather.3.cloned.1.call-start = ((), (), s32[]{:S(2)}) async-start(), calls=%async_computation.9 | async-start | bytes 6684672 | tf_op jit(solution)/shard_map/all_gather | solution.py:110
  8.5 6.3 %copy-start.14 = (f32[192]{0:T(256)}, f32[192]{0:T(256)S(1)}, u32[]{:S(2)}) copy-start(f32[192]{0:T(256)S(1)} %broadcast_multiply_fusion) | copy-start | bytes 2308
  9.8 0.6 copy-start.18
  10.3 4.4 copy-start.16
  17.1 9.8 %copy-start.10 = (bf16[192,8,128]{2,1,0:T(8,128)(2,1)S(1)}, bf16[192,8,128]{2,1,0:T(8,128)(2,1)}, u32[]{:S(2)}) copy-start(bf16[192,8,128]{2,1,0:T(8,128)(2,1)} %get-tuple-element.118) | copy-start | bytes 1179652
  18.8 37.7 %all-to-all-start.2 = ((bf16[16,192,2,1,128]{4,1,3,2,0:T(8,128)(2,1)}), bf16[16,192,2,1,128]{4,1,3,2,0:T(8,128)(2,1)}, u32[]{:S(2)}, u32[]{:S(2)}) async-start(bf16[16,192,2,1,128]{4,1,3,2,0:T(8,128)(2,1)} %bitcast.192), calls=%async_computation.2 | async-start | bytes 3145728 | tf_op jit(solution)/shard_map/all_to_all | solution.py:97
  60.7 4.8 copy-start.4
  60.7 6.3 %copy-start.6 = (bf16[1,192,1024]{2,1,0:T(8,128)(2,1)S(1)}, bf16[1,192,1024]{2,1,0:T(8,128)(2,1)}, u32[]{:S(2)}) copy-start(bf16[1,192,1024]{2,1,0:T(8,128)(2,1)} %param.11) | copy-start | bytes 1179652
  60.7 112.6 %all-to-all-start = ((bf16[16,192,8,128]{3,1,2,0:T(8,128)(2,1)}), bf16[16,192,8,128]{3,1,2,0:T(8,128)(2,1)}, u32[]{:S(2)}, u32[]{:S(2)}) async-start(bf16[16,192,8,128]{3,1,2,0:T(8,128)(2,1)} %stack.12), calls=%async_computation | async-start | bytes 12582912 | tf_op jit(solution)/shard_map/all_to_all | solution.py:11
  67.1 153.3 %copy-start.20 = (f32[192]{0:T(256)}, f32[192]{0:T(256)S(1)}, u32[]{:S(2)}) copy-start(f32[192]{0:T(256)S(1)} %compare_convert_fusion) | copy-start | bytes 2308
  173.3 29.0 %all-to-all-start.1 = ((bf16[16,96,1,128]{3,1,2,0:T(8,128)(2,1)}), bf16[16,96,1,128]{3,1,2,0:T(8,128)(2,1)S(1)}, u32[]{:S(2)}, u32[]{:S(2)}) async-start(bf16[16,96,1,128]{3,1,2,0:T(8,128)(2,1)} %bitcast.196), calls=%async_computation.1 | async-start | bytes 786432 | tf_op jit(solution)/shard_map/all_to_all | solution.py:96
  180.8 3.4 copy-start.5
  202.3 21.6 %all-to-all-start.3 = ((bf16[16,96,1,128]{3,1,2,0:T(8,128)(2,1)}), bf16[16,96,1,128]{3,1,2,0:T(8,128)(2,1)}, u32[]{:S(2)}, u32[]{:S(2)}) async-start(bf16[16,96,1,128]{3,1,2,0:T(8,128)(2,1)} %bitcast.195), calls=%async_computation.3 | async-start | bytes 786432 | tf_op jit(solution)/shard_map/all_to_all | solution.py:139
  209.6 166.2 %reduce-scatter.5.cloned.1.call-start = ((), (), s32[]{:S(2)}) async-start(), calls=%async_computation.8 | async-start | bytes 4456448 | tf_op jit(solution)/shard_map/reduce_scatter | solution.py:131
  209.9 11.3 %copy-start.7 = (bf16[1,192,1024]{2,1,0:T(8,128)(2,1)S(1)}, bf16[1,192,1024]{2,1,0:T(8,128)(2,1)}, u32[]{:S(2)}) copy-start(bf16[1,192,1024]{2,1,0:T(8,128)(2,1)} %param.11) | copy-start | bytes 1179652
  220.4 0.7 copy-start.12
  223.9 239.7 %reduce-scatter.3.cloned.1.call-start = ((), (), s32[]{:S(2)}) async-start(), calls=%async_computation.7 | async-start | bytes 13369344 | tf_op jit(solution)/shard_map/reduce_scatter | solution.py:160
  225.7 2.7 copy-start.1
  229.8 5.9 %copy-start.2 = (f32[512,3072]{1,0:T(8,128)S(1)}, f32[512,3072]{1,0:T(8,128)}, u32[]{:S(2)}) copy-start(f32[512,3072]{1,0:T(8,128)} %copy-done.1) | copy-start | bytes 18874372 | tf_op jit(solution)/shard_map/while
  229.8 5.9 %copy-start.11 = (bf16[3072,128]{1,0:T(8,128)(2,1)S(1)}, bf16[3072,128]{1,0:T(8,128)(2,1)}, u32[]{:S(2)}) copy-start(bf16[3072,128]{1,0:T(8,128)(2,1)} %get-tuple-element.216) | copy-start | bytes 2359300 | tf_op jit(solution)/shard_map/while
  247.4 2.7 copy-start.1
  251.5 6.4 %copy-start.2 = (f32[512,3072]{1,0:T(8,128)S(1)}, f32[512,3072]{1,0:T(8,128)}, u32[]{:S(2)}) copy-start(f32[512,3072]{1,0:T(8,128)} %copy-done.1) | copy-start | bytes 18874372 | tf_op jit(solution)/shard_map/while
  251.5 6.3 %copy-start.11 = (bf16[3072,128]{1,0:T(8,128)(2,1)S(1)}, bf16[3072,128]{1,0:T(8,128)(2,1)}, u32[]{:S(2)}) copy-start(bf16[3072,128]{1,0:T(8,128)(2,1)} %get-tuple-element.216) | copy-start | bytes 2359300 | tf_op jit(solution)/shard_map/while
  271.0 2.7 copy-start.1
  275.1 6.4 %copy-start.2 = (f32[512,3072]{1,0:T(8,128)S(1)}, f32[512,3072]{1,0:T(8,128)}, u32[]{:S(2)}) copy-start(f32[512,3072]{1,0:T(8,128)} %copy-done.1) | copy-start | bytes 18874372 | tf_op jit(solution)/shard_map/while
  275.1 6.4 %copy-start.11 = (bf16[3072,128]{1,0:T(8,128)(2,1)S(1)}, bf16[3072,128]{1,0:T(8,128)(2,1)}, u32[]{:S(2)}) copy-start(bf16[3072,128]{1,0:T(8,128)(2,1)} %get-tuple-element.216) | copy-start | bytes 2359300 | tf_op jit(solution)/shard_map/while
  295.1 37.1 %collective-permute-start = (f32[16,96,2,1,128]{4,1,3,2,0:T(8,128)S(1)}, f32[16,96,2,1,128]{4,1,3,2,0:T(8,128)S(1)}, u32[]{:S(2)}, u32[]{:S(2)}) collective-permute-start(f32[16,96,2,1,128]{4,1,3,2,0:T(8,128)S(1)} %bitcast.194), channel_id=1, source_target_pairs={{0,1},{1,0},{2,3},{3,2},{4,5},{5,4},{6,7},{7,6},{8,9},{9,8},{10,11... | collective-permute-start | bytes 4718600 | tf_op jit(solution)/shard_map/ppermute | solution.py:15
  332.2 29.0 %copy-start.3 = (bf16[1,192,1024]{2,1,0:T(8,128)(2,1)S(1)}, bf16[1,192,1024]{2,1,0:T(8,128)(2,1)}, u32[]{:S(2)}) copy-start(bf16[1,192,1024]{2,1,0:T(8,128)(2,1)} %param.7) | copy-start | bytes 1179652
  332.2 29.0 %copy-start.15 = (f32[192]{0:T(256)S(1)}, f32[192]{0:T(256)}, u32[]{:S(2)}) copy-start(f32[192]{0:T(256)} %copy-done.14) | copy-start | bytes 2308
  332.2 29.0 %copy-start.17 = (f32[192]{0:T(256)S(1)}, f32[192]{0:T(256)}, u32[]{:S(2)}) copy-start(f32[192]{0:T(256)} %copy-done.16) | copy-start | bytes 2308
  369.0 5.6 %copy-start.19 = (f32[192]{0:T(256)S(1)}, f32[192]{0:T(256)}, u32[]{:S(2)}) copy-start(f32[192]{0:T(256)} %copy-done.18) | copy-start | bytes 2308
  369.0 94.7 %copy-start.8 = (bf16[1,192,1024]{2,1,0:T(8,128)(2,1)S(1)}, bf16[1,192,1024]{2,1,0:T(8,128)(2,1)}, u32[]{:S(2)}) copy-start(bf16[1,192,1024]{2,1,0:T(8,128)(2,1)} %param.11) | copy-start | bytes 1179652
  369.0 96.9 %copy-start.13 = (bf16[8,24,8,128]{3,2,1,0:T(8,128)(2,1)S(1)}, bf16[8,24,8,128]{3,2,1,0:T(8,128)(2,1)}, u32[]{:S(2)}) copy-start(bf16[8,24,8,128]{3,2,1,0:T(8,128)(2,1)} %copy-done.12) | copy-start | bytes 1179652
  369.0 96.9 %copy-start.21 = (f32[192]{0:T(256)S(1)}, f32[192]{0:T(256)}, u32[]{:S(2)}) copy-start(f32[192]{0:T(256)} %copy-done.20) | copy-start | bytes 2308
  369.0 158.5 %all-reduce.3.cloned.1.call-start = ((), (), s32[]{:S(2)}) async-start(), calls=%async_computation.10 | async-start | bytes 2097152 | tf_op jit(solution)/shard_map/psum | solution.py:166
  374.6 0.9 copy-start.9
Sparse Core Ops, SparseCore 0:
  17.0 139.6 all-gather.2
  224.0 82.9 reduce-scatter.4
  369.1 94.5 reduce-scatter.2
  465.9 61.5 all-reduce.2
